TPU v7x, 512 devices: a whole 4x8x8 slice. The times are simulated.
512 devices in a mesh: node: 32 (over x, y), tile: 16 (over z, core).
Axes of the slice: x: 4, y: 8, z: 8, core: 2. Of those that a mesh axis runs over, the one named last changes fastest.
Arguments:
- states: bfloat16 [196608, 128], P(('node', 'tile')), may hold values from -6 to 6
- adjacency: bfloat16 [65536, 128, 128], P(('node', 'tile')), may hold values from -0.5 to 0.5
- tile_node: int32 [512, 128], P(('node', 'tile')), may hold values from 0 to 31
- tile_block: int32 [512, 128], P(('node', 'tile')), may hold values from 0 to 1, as said below
- tile_rel: int32 [512, 128], P(('node', 'tile')), may hold values from 0 to 534
- tile_dst: int32 [512, 128], P(('node', 'tile')), may hold values from 0 to 47
- send_blocks: int32 [512, 32, 2], P(('node', 'tile')), may hold values from 0 to 2
- send_count: int32 [512, 32], P(('node', 'tile')), may hold values from 1 to 2, as said below
- active: int32 [2, 1536], P(None, ('node', 'tile')), may hold values 0 or 1
- relations: bfloat16 [535, 128], replicated, may hold values from -6 to 6
- mix_weight: bfloat16 [2, 64, 64], replicated, may hold values from -0.75 to 0.75
- norm_gain: float32 [2, 64], replicated, may hold values from 0.5 to 1.5
Outputs:
- new_states: bfloat16 [196608, 128], P(('node', 'tile'))
Inputs may be any that keep to these rules, and one draw needn't show every extreme that they name: On each device, the first send_count entries of each list are distinct; every device has one list with all 2 slots used. For tile t of device n * 16 + j, tile_block[d, t] is less than send_count[a * 16 + j, n], where a = tile_node[d, t].
All inputs are finite; a program needn't handle non-finite values. No bound on the sum of `active` on one device may be relied on, other than what follows from the above.
Results may differ from a plain program's by a relative error of at most 0.02.
Values may be sent and summed in bfloat16 or wider, within the bound.
No kernel may reach another device: no remote copies, remote signals or barrier semaphores. Data moves between devices by JAX's collectives and lax.ppermute only.
A program may use at most 64 MiB of HBM per device.

v0:
```python
import jax
import jax.numpy as jnp
import numpy as np
from jax import lax
from jax.sharding import Mesh
from jax.sharding import PartitionSpec as P

NODE_AXES = ("x", "y")
TILE_AXES = ("z", "core")
ALL_AXES = NODE_AXES + TILE_AXES


def body(
    states,
    adjacency,
    tile_node,
    tile_block,
    tile_rel,
    tile_dst,
    send_blocks,
    send_count,
    active,
    relations,
    mix_weight,
    norm_gain,
):
    size_block = adjacency.shape[1]
    width = states.shape[1]
    own_blocks = states.shape[0] // size_block
    n_z = lax.axis_size("z")
    n_core = lax.axis_size("core")
    group_blocks = own_blocks * n_z * n_core
    tiles_here = adjacency.shape[0]
    depth = mix_weight.shape[1]
    query_count = width // depth
    me_node = lax.axis_index("x") * lax.axis_size("y") + lax.axis_index("y")
    lists_all = lax.all_gather(send_blocks[0], NODE_AXES, axis=0, tiled=False)
    counts_all = lax.all_gather(send_count[0], NODE_AXES, axis=0, tiled=False)
    lists_mine = lax.dynamic_index_in_dim(lists_all, me_node, axis=1, keepdims=False)
    counts_mine = lax.dynamic_index_in_dim(counts_all, me_node, axis=1, keepdims=False)
    sender = tile_node[0]
    slot = tile_block[0]
    local_block = jnp.clip(lists_mine[sender, slot], 0, own_blocks - 1)
    valid = (slot < counts_mine[sender]).astype(jnp.float32)
    source_index = sender * own_blocks + local_block
    rel_onehot = (
        tile_rel[0][:, None] == jnp.arange(relations.shape[0], dtype=jnp.int32)[None, :]
    ).astype(jnp.bfloat16)
    rel_rows = jnp.dot(rel_onehot, relations, preferred_element_type=jnp.float32)
    rel_rows = rel_rows * valid[:, None]
    dst_onehot = (
        jnp.arange(group_blocks, dtype=jnp.int32)[:, None] == tile_dst[0][None, :]
    ).astype(jnp.bfloat16)
    for layer in range(mix_weight.shape[0]):
        blocks = states.reshape(own_blocks, size_block, width) * active[layer][
            :, None, None
        ].astype(jnp.bfloat16)
        gathered = lax.all_gather(blocks, NODE_AXES, axis=0, tiled=True)
        source_rows = jnp.take(gathered, source_index, axis=0)
        modulated = (source_rows * rel_rows[:, None, :]).astype(jnp.bfloat16)
        products = jnp.einsum(
            "tij,tjf->tif", adjacency, modulated, preferred_element_type=jnp.float32
        )
        flat_products = products.reshape(tiles_here, -1)
        high_part = flat_products.astype(jnp.bfloat16)
        low_part = (flat_products - high_part.astype(jnp.float32)).astype(jnp.bfloat16)
        partial_sum = jnp.dot(dst_onehot, high_part, preferred_element_type=jnp.float32) + jnp.dot(
            dst_onehot, low_part, preferred_element_type=jnp.float32
        )
        partial_sum = partial_sum.astype(jnp.bfloat16).reshape(
            n_z, n_core, own_blocks * size_block, width
        )
        by_core = jnp.swapaxes(partial_sum, 0, 1).reshape(-1, width)
        half = lax.psum_scatter(by_core, "core", scatter_dimension=0, tiled=True)
        summed = lax.psum_scatter(half, "z", scatter_dimension=0, tiled=True)
        mixer = jnp.kron(jnp.eye(query_count, dtype=jnp.bfloat16), mix_weight[layer])
        mixed = jnp.dot(summed, mixer, preferred_element_type=jnp.float32).reshape(
            -1, query_count, depth
        )
        center = jnp.mean(mixed, axis=-1, keepdims=True)
        spread = jnp.mean(jnp.square(mixed - center), axis=-1, keepdims=True)
        normed = (mixed - center) * lax.rsqrt(spread + 1e-05) * norm_gain[layer]
        states = (states.astype(jnp.float32) + jax.nn.relu(normed).reshape(-1, width)).astype(
            jnp.bfloat16
        )
    return states


def solution(mesh):
    n_node, n_tile = mesh.devices.shape
    n_x = 4 if n_node % 4 == 0 else 1
    n_y = n_node // n_x
    fine = Mesh(np.asarray(mesh.devices).reshape(n_x, n_y, n_tile // 2, 2), ALL_AXES)
    rows = P(ALL_AXES, None)
    placed = (
        rows,
        P(ALL_AXES, None, None),
        rows,
        rows,
        rows,
        rows,
        P(ALL_AXES, None, None),
        rows,
        P(None, ALL_AXES),
        P(),
        P(),
        P(),
    )
    return jax.shard_map(body, mesh=fine, in_specs=placed, out_specs=rows, check_vma=False)
```

profile of v0, /device:TPU:2, one launch (start us, length us, event | category | flops | bytes accessed | tf_op | source)
XLA Modules:
  0.0 380.8 jit_solution(17460445903867488199)
XLA Ops:
  6.5 0.7 convert.4
  7.3 1.6 broadcast_multiply_fusion.1
  9.0 40.9 %all_gather.13 = s32[32,32,2]{1,2,0:T(2,128)S(1)} all-gather(s32[1,32,2]{1,2,0:T(2,128)} %param.20), channel_id=1, replica_groups=mesh['x'=4,'y'=8,'z'=8,'core'=2] {'x','y'}, dimensions={0}, use_global_device_ids=true | all-gather | bytes 8448 | tf_op jit(solution)/shard_map/all_gather | solution.py:37
  49.9 0.1 constant_dynamic-slice_fusion
  50.0 0.1 copy.31
  50.1 0.7 fusion.33
  50.8 1.5 gather_fusion
  52.3 33.0 %all-gather = s32[32,1,32]{2,1,0:T(1,128)S(1)} all-gather(s32[1,1,32]{2,1,0:T(1,128)} %bitcast.105), channel_id=1, replica_groups=mesh['x'=4,'y'=8,'z'=8,'core'=2] {'x','y'}, dimensions={0}, use_global_device_ids=true | all-gather | bytes 4224 | tf_op jit(solution)/shard_map/all_gather | solution.py:38
  85.3 0.7 dynamic-slice_reduce_fusion
  86.1 1.2 gather_fusion.1
  87.3 0.7 compare_and_fusion
  88.0 0.7 compare_convert_fusion.1
  88.6 0.9 convolution_multiply_fusion
  89.5 9.0 %all-gather.4.cloned.1.call-done = bf16[96,128,128]{2,1,0:T(8,128)(2,1)} async-done(((bf16[3,128,128]{2,1,0:T(8,128)(2,1)}), bf16[96,128,128]{2,1,0:T(8,128)(2,1)}) %all-gather.4.cloned.1.call-update) | async-done | bytes 3145744 | tf_op jit(solution)/shard_map/all_gather | solution.py:58
  98.6 4.9 %gather_fusion.2 = bf16[128,128,128]{2,1,0:T(8,128)(2,1)} fusion(bf16[96,128,128]{2,1,0:T(8,128)(2,1)} %all-gather.4.cloned.1.call-done, s32[1024]{0:T(1024)S(1)} %pad_clamp_fusion.1), kind=kCustom, calls=%fused_computation.clone | custom fusion | bytes 8389120 | tf_op jit(solution)/shard_map/jit(_take)/gather | solution.py:59
  103.5 9.2 %fusion.13 = f32[128,128,128]{1,2,0:T(8,128)} fusion(bf16[128,128,128]{2,1,0:T(8,128)(2,1)} %param.15, bf16[128,128,128]{2,1,0:T(8,128)(2,1)} %gather_fusion.2, f32[128,128]{1,0:T(8,128)S(1)} %convolution_multiply_fusion, pred[128]{0:T(512)(128)(4,1)S(1)} %get-tuple-element.10), kind=kOutput, calls=%fused_computation.25 | convolution fusion | flops 545259520 | bytes 16842880 | tf_op jit(solution)/shard_map/tij,tjf->tif/dot_general | solution.py:61
  112.7 9.3 %copy.33 = f32[128,128,128]{0,2,1:T(8,128)} copy(f32[128,128,128]{1,2,0:T(8,128)} %fusion.13) | data formatting | bytes 16777216 | tf_op jit(solution)/shard_map/tij,tjf->tif/dot_general | solution.py:61
  122.1 4.0 %fusion.3 = (bf16[128,16384]{0,1:T(8,128)(2,1)S(1)}, bf16[128,16384]{0,1:T(8,128)(2,1)S(1)}) fusion(f32[128,128,128]{0,2,1:T(8,128)} %copy.33), kind=kLoop, calls=%fused_computation.13 | loop fusion | flops 8388608 | bytes 16777216 | tf_op jit(solution)/shard_map/convert_element_type | solution.py:66
  126.1 1.5 fusion.22
  127.7 1.5 fusion
  129.2 0.8 reshape.172
  130.0 1.3 copy.34
  131.4 15.8 %reduce-scatter.5.cloned.1.call-done = bf16[3072,128]{1,0:T(8,128)(2,1)} async-done(((bf16[6144,128]{1,0:T(8,128)(2,1)}), bf16[3072,128]{1,0:T(8,128)(2,1)}) %reduce-scatter.5.cloned.1.call-update) | async-done | bytes 786448 | tf_op jit(solution)/shard_map/reduce_scatter | solution.py:74
  147.2 0.1 copy.35
  147.3 0.1 copy.40
  147.4 0.2 broadcast_multiply_fusion.3
  147.6 0.1 mul.145
  147.7 45.3 %reduce-scatter.7.cloned.1.call-done = bf16[384,128]{1,0:T(8,128)(2,1)} async-done(((bf16[3072,128]{1,0:T(8,128)(2,1)}), bf16[384,128]{1,0:T(8,128)(2,1)}) %reduce-scatter.7.cloned.1.call-update) | async-done | bytes 98320 | tf_op jit(solution)/shard_map/reduce_scatter | solution.py:75
  193.1 1.1 fusion.34
  194.2 0.1 multiply_maximum_fusion.1
  194.3 0.1 copy.36
  194.5 0.7 broadcast_multiply_fusion
  195.2 0.2 reduce-scatter.9.cloned.1.call-start
  195.5 82.1 %all-gather.6.cloned.1.call-done = bf16[96,128,128]{2,1,0:T(8,128)(2,1)} async-done(((bf16[3,128,128]{2,1,0:T(8,128)(2,1)}), bf16[96,128,128]{2,1,0:T(8,128)(2,1)}) %all-gather.6.cloned.1.call-update) | async-done | bytes 3145744 | tf_op jit(solution)/shard_map/all_gather | solution.py:58
  277.6 4.9 %gather_fusion.3 = bf16[128,128,128]{2,1,0:T(8,128)(2,1)} fusion(bf16[96,128,128]{2,1,0:T(8,128)(2,1)} %all-gather.6.cloned.1.call-done, s32[1024]{0:T(1024)S(1)} %pad_clamp_fusion.1), kind=kCustom, calls=%fused_computation.1.clone | custom fusion | bytes 8389120 | tf_op jit(solution)/shard_map/jit(_take)/gather | solution.py:59
  282.5 9.2 %fusion.12 = f32[128,128,128]{1,2,0:T(8,128)} fusion(bf16[128,128,128]{2,1,0:T(8,128)(2,1)} %param.15, bf16[128,128,128]{2,1,0:T(8,128)(2,1)} %gather_fusion.3, f32[128,128]{1,0:T(8,128)S(1)} %convolution_multiply_fusion, pred[128]{0:T(512)(128)(4,1)S(1)} %get-tuple-element.10), kind=kOutput, calls=%fused_computation.24 | convolution fusion | flops 545259520 | bytes 16842880 | tf_op jit(solution)/shard_map/tij,tjf->tif/dot_general | solution.py:61
  291.8 9.3 %copy.38 = f32[128,128,128]{0,2,1:T(8,128)} copy(f32[128,128,128]{1,2,0:T(8,128)} %fusion.12) | data formatting | bytes 16777216 | tf_op jit(solution)/shard_map/tij,tjf->tif/dot_general | solution.py:61
  301.1 4.0 %fusion.2 = (bf16[128,16384]{0,1:T(8,128)(2,1)S(1)}, bf16[128,16384]{0,1:T(8,128)(2,1)S(1)}) fusion(f32[128,128,128]{0,2,1:T(8,128)} %copy.38), kind=kLoop, calls=%fused_computation.10 | loop fusion | flops 8388608 | bytes 16777216 | tf_op jit(solution)/shard_map/convert_element_type | solution.py:66
  305.1 1.5 fusion.21
  306.7 1.5 fusion.1
  308.2 0.8 reshape.177
  309.0 1.3 copy.39
  310.4 15.7 %reduce-scatter.9.cloned.1.call-done = bf16[3072,128]{1,0:T(8,128)(2,1)} async-done(((bf16[6144,128]{1,0:T(8,128)(2,1)}), bf16[3072,128]{1,0:T(8,128)(2,1)}) %reduce-scatter.9.cloned.1.call-update) | async-done | bytes 786448 | tf_op jit(solution)/shard_map/reduce_scatter | solution.py:74
  326.1 0.1 mul.157
  326.2 45.7 %reduce-scatter.11.cloned.1.call-done = bf16[384,128]{1,0:T(8,128)(2,1)} async-done(((bf16[3072,128]{1,0:T(8,128)(2,1)}), bf16[384,128]{1,0:T(8,128)(2,1)}) %reduce-scatter.11.cloned.1.call-update) | async-done | bytes 98320 | tf_op jit(solution)/shard_map/reduce_scatter | solution.py:75
  371.9 1.1 fusion.35
  373.2 0.1 copy.41
  373.3 0.7 add_convert_fusion
  (37 shorter events, 0.6 us)
Async XLA Ops:
  6.5 82.1 %copy-start = (bf16[535,128]{1,0:T(8,128)(2,1)S(1)}, bf16[535,128]{1,0:T(8,128)(2,1)}, u32[]{:S(2)}) copy-start(bf16[535,128]{1,0:T(8,128)(2,1)} %param.23) | copy-start | bytes 410884
  6.5 92.0 %all-gather.4.cloned.1.call-start = ((), (), s32[]{:S(2)}) async-start(), calls=%async_computation.4 | async-start | bytes 3244032 | tf_op jit(solution)/shard_map/all_gather | solution.py:58
  8.9 138.2 %reduce-scatter.5.cloned.1.call-start = ((), (), s32[]{:S(2)}) async-start(), calls=%async_computation.5 | async-start | bytes 2359296 | tf_op jit(solution)/shard_map/reduce_scatter | solution.py:74
  122.1 4.0 %copy-start.4 = (s32[1,128]{1,0:T(1,128)S(1)}, s32[1,128]{1,0:T(1,128)}, u32[]{:S(2)}) copy-start(s32[1,128]{1,0:T(1,128)} %param.19) | copy-start | bytes 1540
  129.2 18.0 %copy-start.3 = (bf16[2,64,64]{2,1,0:T(8,128)(2,1)S(1)}, bf16[2,64,64]{2,1,0:T(8,128)(2,1)}, u32[]{:S(2)}) copy-start(bf16[2,64,64]{2,1,0:T(8,128)(2,1)} %param.24) | copy-start | bytes 49156
  129.2 18.5 %copy-start.5 = (f32[2,64]{1,0:T(2,128)S(1)}, f32[2,64]{1,0:T(2,128)}, u32[]{:S(2)}) copy-start(f32[2,64]{1,0:T(2,128)} %param.25) | copy-start | bytes 1540
  130.0 64.4 %copy-start.2 = (bf16[384,128]{1,0:T(8,128)(2,1)S(1)}, bf16[384,128]{1,0:T(8,128)(2,1)}, u32[]{:S(2)}) copy-start(bf16[384,128]{1,0:T(8,128)(2,1)} %param.14) | copy-start | bytes 294916
  131.3 61.7 %reduce-scatter.7.cloned.1.call-start = ((), (), s32[]{:S(2)}) async-start(), calls=%async_computation.6 | async-start | bytes 884736 | tf_op jit(solution)/shard_map/reduce_scatter | solution.py:75
  147.2 130.5 %all-gather.6.cloned.1.call-start = ((), (), s32[]{:S(2)}) async-start(), calls=%async_computation.7 | async-start | bytes 3244032 | tf_op jit(solution)/shard_map/all_gather | solution.py:58
  195.2 130.9 %reduce-scatter.9.cloned.1.call-start = ((), (), s32[]{:S(2)}) async-start(), calls=%async_computation.8 | async-start | bytes 2359296 | tf_op jit(solution)/shard_map/reduce_scatter | solution.py:74
  308.2 65.7 %copy-start.1 = (bf16[535,128]{1,0:T(8,128)(2,1)S(1)}, bf16[535,128]{1,0:T(8,128)(2,1)}, u32[]{:S(2)}) copy-start(bf16[535,128]{1,0:T(8,128)(2,1)} %param.23) | copy-start | bytes 410884
  310.3 61.6 %reduce-scatter.11.cloned.1.call-start = ((), (), s32[]{:S(2)}) async-start(), calls=%async_computation.9 | async-start | bytes 884736 | tf_op jit(solution)/shard_map/reduce_scatter | solution.py:75
Sparse Core Ops, SparseCore 0:
  10.5 88.0 all-gather.3
  131.4 15.6 reduce-scatter.4
  150.0 43.0 reduce-scatter.6
  196.1 81.4 all-gather.5
  310.4 15.6 reduce-scatter.8
  328.8 43.0 reduce-scatter.10
where the time goes:
time: 381 us
  waiting for transfers between devices  214 us (56%)
  blocking collectives  74 us (19%)
  local copies, waits for them, and re-layouts  36.9 us (10%)
  matrix products  27.7 us (7%)
  other arithmetic  14.3 us (4%)
  between operations  13.8 us (4%)
    all_gather x2, waiting for transfers between devices, body(): gathered = lax.all_gather(blocks, NODE_AXES, axis=0, tiled=True)  91.2 us
    reduce_scatter x2, waiting for transfers between devices, body(): summed = lax.psum_scatter(half, 'z', scatter_dimension=0, tiled=True)  91 us
    all_gather x1, blocking collectives, body(): lists_all = lax.all_gather(send_blocks[0], NODE_AXES, axis=0, tiled=False)  40.9 us
    all_gather x1, blocking collectives, body(): counts_all = lax.all_gather(send_count[0], NODE_AXES, axis=0, tiled=False)  33 us
    reduce_scatter x2, waiting for transfers between devices, body(): half = lax.psum_scatter(by_core, 'core', scatter_dimension=0, tiled=True)  31.5 us
    dot_general x2, local copies, waits for them, and re-layouts, body(): jnp.einsum('tij,tjf->tif', adjacency, modulated, preferred_element_type=j...  18.6 us
    dot_general x2, matrix products, body(): jnp.einsum('tij,tjf->tif', adjacency, modulated, preferred_element_type=j...  18.5 us
    gather x2, local copies, waits for them, and re-layouts, body(): source_rows = jnp.take(gathered, source_index, axis=0)  9.87 us
  transfers between devices with their start and end apart: 6, of which 6 were waited for; matrix products, arithmetic and copies ran while one was open for 2% of the time, Pallas kernels for 0%

commit v1 on v0

--- a/solution.py
+++ b/solution.py
@@ -55,7 +55,10 @@
         blocks = states.reshape(own_blocks, size_block, width) * active[layer][
             :, None, None
         ].astype(jnp.bfloat16)
-        gathered = lax.all_gather(blocks, NODE_AXES, axis=0, tiled=True)
+        w2 = lax.all_to_all(
+            jnp.stack([blocks for _ in range(lax.axis_size(NODE_AXES))]), NODE_AXES, 0, 0
+        )
+        gathered = jnp.concatenate(w2, 0)
         source_rows = jnp.take(gathered, source_index, axis=0)
         modulated = (source_rows * rel_rows[:, None, :]).astype(jnp.bfloat16)
         products = jnp.einsum(

time: 381 us -> 433 us (1.14)
  blocking collectives: 74 us -> 210 us
  waiting for transfers between devices: 214 us -> 124 us
  starting transfers between devices: 0.39 us -> 10.5 us
    all_gather x2 -> x0, waiting for transfers between devices: 91.2 us -> none  [body(): gathered = lax.all_gather(blocks, NODE_AXES, axis=0, tiled=True)]
    all_to_all x0 -> x1, blocking collectives: none -> 75.7 us  [body(): lax.all_to_all(jnp.stack([blocks for _ in range(lax.axis_size(NODE_AXES))...]
    all_gather x1, blocking collectives: 40.9 us -> 102 us  [body(): lists_all = lax.all_gather(send_blocks[0], NODE_AXES, axis=0, tiled=False)]
    all_to_all x0 -> x1, starting transfers between devices: none -> 10.4 us  [body(): lax.all_to_all(jnp.stack([blocks for _ in range(lax.axis_size(NODE_AXES))...]
  transfers between devices with their start and end apart: 6 -> 5, of which waited for: 6 -> 4; matrix products, arithmetic and copies ran while one was open for 2% -> 1% of each run, Pallas kernels for 0% -> 0%
where the time goes in v1:
time: 433 us
  blocking collectives  210 us (48%)
  waiting for transfers between devices  124 us (29%)
  local copies, waits for them, and re-layouts  36.5 us (8%)
  matrix products  27.1 us (6%)
  between operations  13.5 us (3%)
  other arithmetic  11 us (3%)
  starting transfers between devices  10.5 us (2%)
    all_gather x1, blocking collectives, body(): lists_all = lax.all_gather(send_blocks[0], NODE_AXES, axis=0, tiled=False)  102 us
    reduce_scatter x2, waiting for transfers between devices, body(): summed = lax.psum_scatter(half, 'z', scatter_dimension=0, tiled=True)  91 us
    all_to_all x1, blocking collectives, body(): lax.all_to_all(jnp.stack([blocks for _ in range(lax.axis_size(NODE_AXES))...  75.7 us
    reduce_scatter x2, waiting for transfers between devices, body(): half = lax.psum_scatter(by_core, 'core', scatter_dimension=0, tiled=True)  32.9 us
    all_gather x1, blocking collectives, body(): counts_all = lax.all_gather(send_count[0], NODE_AXES, axis=0, tiled=False)  32.5 us
    dot_general x2, local copies, waits for them, and re-layouts, body(): jnp.einsum('tij,tjf->tif', adjacency, modulated, preferred_element_type=j...  18.8 us
    dot_general x2, matrix products, body(): jnp.einsum('tij,tjf->tif', adjacency, modulated, preferred_element_type=j...  18.4 us
    all_to_all x1, starting transfers between devices, body(): lax.all_to_all(jnp.stack([blocks for _ in range(lax.axis_size(NODE_AXES))...  10.4 us
  transfers between devices with their start and end apart: 5, of which 4 were waited for; matrix products, arithmetic and copies ran while one was open for 1% of the time, Pallas kernels for 0%

profile of v1, /device:TPU:2, one launch (start us, length us, event | category | flops | bytes accessed | tf_op | source)
XLA Modules:
  0.0 432.8 jit_solution(3218005651048108618)
XLA Ops:
  6.5 0.7 convert.4
  7.3 1.0 broadcast_multiply_fusion.1
  8.3 2.4 stack.4
  10.7 10.4 %all-to-all-start = ((bf16[32,3,128,128]{3,2,1,0:T(8,128)(2,1)}), bf16[32,3,128,128]{3,2,1,0:T(8,128)(2,1)S(1)}, u32[]{:S(2)}, u32[]{:S(2)}) async-start(bf16[32,3,128,128]{3,2,1,0:T(8,128)(2,1)} %stack.4), calls=%async_computation | async-start | bytes 6291456 | tf_op jit(solution)/shard_map/all_to_all | solution.py:58
  21.1 0.0 reduce-scatter.5.cloned.1.call-start
  21.1 101.9 %all_gather.6 = s32[32,32,2]{1,2,0:T(2,128)S(1)} all-gather(s32[1,32,2]{1,2,0:T(2,128)S(1)} %copy-done.6), channel_id=1, replica_groups=mesh['x'=4,'y'=8,'z'=8,'core'=2] {'x','y'}, dimensions={0}, use_global_device_ids=true | all-gather | bytes 8448 | tf_op jit(solution)/shard_map/all_gather | solution.py:37
  123.1 0.1 constant_dynamic-slice_fusion
  123.2 0.1 copy.31
  123.3 1.5 gather_fusion
  124.8 32.5 %all-gather = s32[32,1,32]{2,1,0:T(1,128)S(1)} all-gather(s32[1,1,32]{2,1,0:T(1,128)S(1)} %bitcast.109), channel_id=1, replica_groups=mesh['x'=4,'y'=8,'z'=8,'core'=2] {'x','y'}, dimensions={0}, use_global_device_ids=true | all-gather | bytes 4224 | tf_op jit(solution)/shard_map/all_gather | solution.py:38
  157.3 0.7 dynamic-slice_reduce_fusion
  158.1 1.2 gather_fusion.1
  159.4 0.2 convolution_multiply_fusion
  159.6 3.0 gather_fusion.2
  162.7 9.2 %fusion.13 = f32[128,128,128]{1,2,0:T(8,128)} fusion(bf16[128,128,128]{2,1,0:T(8,128)(2,1)} %param.15, bf16[128,128,128]{2,1,0:T(8,128)(2,1)} %gather_fusion.2, f32[128,128]{1,0:T(8,128)S(1)} %convolution_multiply_fusion, pred[128]{0:T(512)(128)(4,1)S(1)} %get-tuple-element.10), kind=kOutput, calls=%fused_computation.25 | convolution fusion | flops 545259520 | bytes 16842880 | tf_op jit(solution)/shard_map/tij,tjf->tif/dot_general | solution.py:64
  171.9 9.4 %copy.33 = f32[128,128,128]{0,2,1:T(8,128)} copy(f32[128,128,128]{1,2,0:T(8,128)} %fusion.13) | data formatting | bytes 16777216 | tf_op jit(solution)/shard_map/tij,tjf->tif/dot_general | solution.py:64
  181.3 4.0 fusion.3
  185.4 1.5 fusion.22
  186.9 1.5 fusion
  188.5 0.8 reshape.185
  189.3 1.3 copy.34
  190.6 19.4 %reduce-scatter.5.cloned.1.call-done = bf16[3072,128]{1,0:T(8,128)(2,1)} async-done(((bf16[6144,128]{1,0:T(8,128)(2,1)}), bf16[3072,128]{1,0:T(8,128)(2,1)}) %reduce-scatter.5.cloned.1.call-update) | async-done | bytes 786448 | tf_op jit(solution)/shard_map/reduce_scatter | solution.py:77
  210.2 0.1 copy.35
  210.3 0.1 copy.40
  210.4 0.2 broadcast_multiply_fusion.3
  210.6 0.1 mul.149
  210.7 45.3 %reduce-scatter.7.cloned.1.call-done = bf16[384,128]{1,0:T(8,128)(2,1)} async-done(((bf16[3072,128]{1,0:T(8,128)(2,1)}), bf16[384,128]{1,0:T(8,128)(2,1)}) %reduce-scatter.7.cloned.1.call-update) | async-done | bytes 98320 | tf_op jit(solution)/shard_map/reduce_scatter | solution.py:78
  256.0 1.1 fusion.34
  257.2 0.1 multiply_maximum_fusion.1
  257.3 0.1 copy.36
  257.4 0.1 broadcast_multiply_fusion
  257.5 0.8 stack.5
  258.3 75.7 %all_to_all.10 = bf16[32,3,128,128]{3,2,1,0:T(8,128)(2,1)S(1)} all-to-all(bf16[32,3,128,128]{3,2,1,0:T(8,128)(2,1)S(1)} %stack.5), channel_id=1, replica_groups=mesh['x'=4,'y'=8,'z'=8,'core'=2] {'x','y'}, dimensions={0} | all-to-all | bytes 6291456 | tf_op jit(solution)/shard_map/all_to_all | solution.py:58
  334.0 3.0 gather_fusion.3
  337.0 9.2 %fusion.12 = f32[128,128,128]{1,2,0:T(8,128)} fusion(bf16[128,128,128]{2,1,0:T(8,128)(2,1)} %param.15, bf16[128,128,128]{2,1,0:T(8,128)(2,1)} %gather_fusion.3, f32[128,128]{1,0:T(8,128)S(1)} %convolution_multiply_fusion, pred[128]{0:T(512)(128)(4,1)S(1)} %get-tuple-element.10), kind=kOutput, calls=%fused_computation.24 | convolution fusion | flops 545259520 | bytes 16842880 | tf_op jit(solution)/shard_map/tij,tjf->tif/dot_general | solution.py:64
  346.3 9.4 %copy.38 = f32[128,128,128]{0,2,1:T(8,128)} copy(f32[128,128,128]{1,2,0:T(8,128)} %fusion.12) | data formatting | bytes 16777216 | tf_op jit(solution)/shard_map/tij,tjf->tif/dot_general | solution.py:64
  355.7 4.0 fusion.2
  359.7 1.5 fusion.21
  361.2 1.5 fusion.1
  362.8 0.8 reshape.191
  363.6 1.3 copy.39
  364.9 13.5 %reduce-scatter.9.cloned.1.call-done = bf16[3072,128]{1,0:T(8,128)(2,1)} async-done(((bf16[6144,128]{1,0:T(8,128)(2,1)}), bf16[3072,128]{1,0:T(8,128)(2,1)}) %reduce-scatter.9.cloned.1.call-update) | async-done | bytes 786448 | tf_op jit(solution)/shard_map/reduce_scatter | solution.py:77
  378.4 0.1 mul.161
  378.5 45.6 %reduce-scatter.11.cloned.1.call-done = bf16[384,128]{1,0:T(8,128)(2,1)} async-done(((bf16[3072,128]{1,0:T(8,128)(2,1)}), bf16[384,128]{1,0:T(8,128)(2,1)}) %reduce-scatter.11.cloned.1.call-update) | async-done | bytes 98320 | tf_op jit(solution)/shard_map/reduce_scatter | solution.py:78
  424.2 1.1 fusion.35
  425.3 0.1 multiply_maximum_fusion
  425.4 0.1 copy.41
  425.6 0.7 add_convert_fusion
  (46 shorter events, 0.4 us)
Async XLA Ops:
  6.5 152.8 %copy-start = (bf16[535,128]{1,0:T(8,128)(2,1)S(1)}, bf16[535,128]{1,0:T(8,128)(2,1)}, u32[]{:S(2)}) copy-start(bf16[535,128]{1,0:T(8,128)(2,1)} %param.23) | copy-start | bytes 410884
  8.2 12.9 %copy-start.6 = (s32[1,32,2]{1,2,0:T(2,128)S(1)}, s32[1,32,2]{1,2,0:T(2,128)}, u32[]{:S(2)}) copy-start(s32[1,32,2]{1,2,0:T(2,128)} %param.20) | copy-start | bytes 772
  8.2 115.0 %copy-start.5 = (s32[1,128]{1,0:T(1,128)S(1)}, s32[1,128]{1,0:T(1,128)}, u32[]{:S(2)}) copy-start(s32[1,128]{1,0:T(1,128)} %param.16) | copy-start | bytes 1540
  8.3 115.0 %copy-start.9 = (s32[1,128]{1,0:T(1,128)S(1)}, s32[1,128]{1,0:T(1,128)}, u32[]{:S(2)}) copy-start(s32[1,128]{1,0:T(1,128)} %param.17) | copy-start | bytes 1540
  10.7 114.1 %copy-start.8 = (s32[1,32]{1,0:T(1,128)S(1)}, s32[1,32]{1,0:T(1,128)}, u32[]{:S(2)}) copy-start(s32[1,32]{1,0:T(1,128)} %param.21) | copy-start | bytes 388
  10.7 148.7 %copy-start.10 = (s32[1,128]{1,0:T(1,128)S(1)}, s32[1,128]{1,0:T(1,128)}, u32[]{:S(2)}) copy-start(s32[1,128]{1,0:T(1,128)} %param.18) | copy-start | bytes 1540
  10.7 148.9 %all-to-all-start = ((bf16[32,3,128,128]{3,2,1,0:T(8,128)(2,1)}), bf16[32,3,128,128]{3,2,1,0:T(8,128)(2,1)S(1)}, u32[]{:S(2)}, u32[]{:S(2)}) async-start(bf16[32,3,128,128]{3,2,1,0:T(8,128)(2,1)} %stack.4), calls=%async_computation | async-start | bytes 6291456 | tf_op jit(solution)/shard_map/all_to_all | solution.py:58
  21.1 189.0 %reduce-scatter.5.cloned.1.call-start = ((), (), s32[]{:S(2)}) async-start(), calls=%async_computation.6 | async-start | bytes 2359296 | tf_op jit(solution)/shard_map/reduce_scatter | solution.py:77
  181.3 4.0 copy-start.4
  188.5 21.7 %copy-start.3 = (bf16[2,64,64]{2,1,0:T(8,128)(2,1)S(1)}, bf16[2,64,64]{2,1,0:T(8,128)(2,1)}, u32[]{:S(2)}) copy-start(bf16[2,64,64]{2,1,0:T(8,128)(2,1)} %param.24) | copy-start | bytes 49156
  188.5 22.2 %copy-start.7 = (f32[2,64]{1,0:T(2,128)S(1)}, f32[2,64]{1,0:T(2,128)}, u32[]{:S(2)}) copy-start(f32[2,64]{1,0:T(2,128)} %param.25) | copy-start | bytes 1540
  189.3 68.1 %copy-start.2 = (bf16[384,128]{1,0:T(8,128)(2,1)S(1)}, bf16[384,128]{1,0:T(8,128)(2,1)}, u32[]{:S(2)}) copy-start(bf16[384,128]{1,0:T(8,128)(2,1)} %param.14) | copy-start | bytes 294916
  190.6 65.4 %reduce-scatter.7.cloned.1.call-start = ((), (), s32[]{:S(2)}) async-start(), calls=%async_computation.7 | async-start | bytes 884736 | tf_op jit(solution)/shard_map/reduce_scatter | solution.py:78
  210.1 168.3 %reduce-scatter.9.cloned.1.call-start = ((), (), s32[]{:S(2)}) async-start(), calls=%async_computation.8 | async-start | bytes 2359296 | tf_op jit(solution)/shard_map/reduce_scatter | solution.py:77
  362.8 63.4 %copy-start.1 = (bf16[535,128]{1,0:T(8,128)(2,1)S(1)}, bf16[535,128]{1,0:T(8,128)(2,1)}, u32[]{:S(2)}) copy-start(bf16[535,128]{1,0:T(8,128)(2,1)} %param.23) | copy-start | bytes 410884
  364.9 59.3 %reduce-scatter.11.cloned.1.call-start = ((), (), s32[]{:S(2)}) async-start(), calls=%async_computation.9 | async-start | bytes 884736 | tf_op jit(solution)/shard_map/reduce_scatter | solution.py:78
Sparse Core Ops, SparseCore 0:
  190.7 19.3 reduce-scatter.4
  212.9 43.0 reduce-scatter.6
  365.0 13.3 reduce-scatter.8
  381.1 43.0 reduce-scatter.10
